TPU v7x, 512 devices: a whole 4x8x8 slice. The times are simulated.
512 devices in a mesh: src: 32 (over y, x_lo, core), rcv: 8 (over z), int: 2 (over x_hi).
Axes of the slice: x: 4 (x_hi: 2, x_lo: 2; x = x_hi * 2 + x_lo), y: 8, z: 8, core: 2. Of those that a mesh axis runs over, the one named last changes fastest.
Arguments:
- traces: float32 [2, 1, 4096, 4096], P(None, None, 'src', 'rcv'), may hold values from -6 to 6
- missing: int32 [32, 32], P('src', 'rcv'), may hold values from 0 to 1, as said below
- aperture: int32 [32, 24], P('src'), may hold values from 0 to 32, as said below
- wavelet: float32 [2, 1], replicated, may hold values from -0.06 to 0.06
Outputs:
- primaries: float32 [2, 1, 4096, 4096], P(None, None, 'src', ('rcv', 'int'))
Inputs may be any that keep to these rules, and one draw needn't show every extreme that they name: `missing`: A tile is marked only where its receiver block lies above its source block, so the mirrored tile is always recorded; some tile is marked. `aperture`: in each row the listed blocks come first and are distinct; the remaining entries are the padding value 32. Each row lists 24 // 2 to 24 blocks; some row lists exactly 24 and some row exactly 12.
All inputs are finite; a program needn't handle non-finite values.
Results may differ from a plain program's by a relative error of at most 0.00005.
Values sent between devices are 32-bit elements; how exact they have to be, the bound alone decides.
No kernel may reach another device: no remote copies, remote signals or barrier semaphores. Data moves between devices by JAX's collectives and lax.ppermute only.
A program may use at most 64 MiB of HBM per device.

v0:
```python
import jax
import jax.numpy as jnp
import numpy as np
from jax import lax
from jax.sharding import Mesh
from jax.sharding import PartitionSpec as P

TILE = 128
SRC = ("y", "xl", "c")
FILL = ("y", "xl", "c", "z")


def mirror_pairs(n_src, n_rcv, per_rcv, step):
    pairs = []
    for s in range(n_src):
        for r in range(n_rcv):
            t = (s % per_rcv + step) % per_rcv
            dest_s = per_rcv * r + t
            if s > dest_s:
                pairs.append((s * n_rcv + r, dest_s * n_rcv + s // per_rcv))
    return pairs


def per_device(traces, missing, aperture, wavelet):
    n_src = lax.axis_size(SRC)
    n_rcv = lax.axis_size("z")
    n_half = lax.axis_size("xh")
    n_core = lax.axis_size("c")
    me_src = lax.axis_index(SRC)
    me_rcv = lax.axis_index("z")
    my_half = lax.axis_index("xh")
    comp_count, freq_count, local_rows, local_cols = traces.shape
    assert local_rows == TILE
    per_rcv = local_cols // TILE
    tiles = traces.reshape(comp_count, freq_count, TILE, per_rcv, TILE)
    arrived = []
    for step in range(per_rcv):
        pick = (me_src % per_rcv + step) % per_rcv
        sent = lax.dynamic_index_in_dim(tiles, pick, 3, keepdims=False)
        got = lax.ppermute(sent, FILL, mirror_pairs(n_src, n_rcv, per_rcv, step))
        arrived.append(jnp.swapaxes(got, 2, 3))
    arrived = jnp.stack(arrived, axis=3)
    order = (me_src % per_rcv - jnp.arange(per_rcv)) % per_rcv
    mirrored = jnp.take(arrived, order, axis=3)
    marks = (missing[0] > 0)[None, None, None, :, None]
    filled = jnp.where(marks, mirrored, tiles)
    first = me_rcv * per_rcv
    local_blocks = first + jnp.arange(per_rcv, dtype=jnp.int32)
    chosen = (aperture[0][:, None] == local_blocks[None, :]).astype(jnp.float32).sum(axis=0)
    half = TILE // n_half
    left = filled.reshape(comp_count, freq_count, TILE, per_rcv, n_half, half)
    left = lax.dynamic_index_in_dim(left, my_half, 4, keepdims=False)
    left = left * chosen[None, None, None, :, None]
    left = left.reshape(comp_count, freq_count, TILE, per_rcv * half)
    left = lax.all_gather(left, "z", axis=3, tiled=True)
    n_pair = n_src // n_core
    left = left.reshape(comp_count, freq_count, TILE, n_pair, n_core, half)
    left = jnp.transpose(left, (1, 0, 2, 4, 3, 5))
    left = left.reshape(freq_count, comp_count * TILE, n_src * half)
    right = filled.reshape(comp_count, freq_count, n_half, half, local_cols)
    right = lax.dynamic_index_in_dim(right, my_half, 2, keepdims=False)
    right = jnp.transpose(right, (1, 2, 0, 3))
    right = lax.all_gather(right, ("y", "xl"), axis=1, tiled=True)
    right = lax.all_gather(right, "c", axis=1, tiled=False)
    right = right.reshape(freq_count, n_src * half, comp_count * local_cols)
    prod = jnp.einsum("fak,fkb->fab", left, right, precision=lax.Precision.HIGHEST)
    prod = prod.reshape(freq_count, comp_count, TILE, comp_count, local_cols)
    real_part = prod[:, 0, :, 0] - prod[:, 1, :, 1]
    imag_part = prod[:, 0, :, 1] + prod[:, 1, :, 0]
    partial_sum = jnp.stack([real_part, imag_part])
    my_share = lax.psum_scatter(partial_sum, "xh", scatter_dimension=3, tiled=True)
    out_cols = local_cols // n_half
    kept = filled.reshape(comp_count, freq_count, TILE, local_cols)
    kept = lax.dynamic_slice_in_dim(kept, my_half * out_cols, out_cols, axis=3)
    w_real = wavelet[0][:, None, None]
    w_imag = wavelet[1][:, None, None]
    out_real = kept[0] - (w_real * my_share[0] - w_imag * my_share[1])
    out_imag = kept[1] - (w_real * my_share[1] + w_imag * my_share[0])
    return jnp.stack([out_real, out_imag])


def solution(mesh):
    n_src, n_rcv, n_int = (mesh.shape[a] for a in ("src", "rcv", "int"))
    fine = Mesh(
        np.asarray(mesh.devices).reshape(n_src // 4, 2, 2, n_rcv, n_int),
        ("y", "xl", "c", "z", "xh"),
    )
    placed = (P(None, None, SRC, "z"), P(SRC, "z"), P(SRC, None), P())
    return jax.shard_map(
        per_device,
        mesh=fine,
        in_specs=placed,
        out_specs=P(None, None, SRC, ("z", "xh")),
        check_vma=False,
    )
```

profile of v0, /device:TPU:1, one launch (start us, length us, event | category | flops | bytes accessed | tf_op | source)
XLA Modules:
  0.0 325.5 jit_solution(12362574936343730955)
XLA Ops:
  6.5 1.3 reshape.249
  7.8 0.5 constant_dynamic-slice_fusion.3
  8.4 8.8 %collective-permute-start.3 = (f32[2,1,128,128]{2,3,0,1:T(8,128)S(1)}, f32[2,1,128,128]{2,3,0,1:T(8,128)S(1)}, u32[]{:S(2)}, u32[]{:S(2)}) collective-permute-start(f32[2,1,128,128]{2,3,0,1:T(8,128)S(1)} %bitcast.75), channel_id=1, source_target_pairs={{16,0},{32,16},{48,32},{64,50},{80,2},{82,66},{96,18},{98,82},{112... | collective-permute-start | bytes 393224 | tf_op jit(solution)/shard_map/ppermute | solution.py:40
  17.3 0.7 collective-permute-start.1
  18.1 1.3 collective-permute-start.2
  19.5 0.7 collective-permute-start
  20.2 0.7 compare_bitcast_fusion
  21.0 4.1 %collective-permute-done.2 = f32[2,1,128,128]{2,3,0,1:T(8,128)S(1)} collective-permute-done((f32[2,1,128,128]{2,3,0,1:T(8,128)S(1)}, f32[2,1,128,128]{2,3,0,1:T(8,128)S(1)}, u32[]{:S(2)}, u32[]{:S(2)}) %collective-permute-start.2) | collective-permute-done | bytes 131104 | tf_op jit(solution)/shard_map/ppermute | solution.py:40
  25.1 0.6 gather_fusion
  25.7 0.3 copy.42
  26.1 0.2 gather.13
  26.3 1.7 fusion.2
  28.1 0.2 copy.44
  28.3 0.2 convert_reduce_fusion
  28.7 0.2 copy.43
  28.9 0.1 dynamic-slice_select_fusion.2
  29.0 0.8 bitcast_multiply_fusion
  29.8 138.6 %all-gather.7.cloned.1.call-done = f32[1,1024,2,512]{3,1,2,0:T(8,128)} async-done(((f32[1,64,2,512]{3,1,2,0:T(8,128)}), f32[1,1024,2,512]{3,1,2,0:T(8,128)}) %all-gather.7.cloned.1.call-update) | async-done | bytes 4194320 | tf_op jit(solution)/shard_map/all_gather | solution.py:63
  168.5 0.2 reduce-scatter.2.cloned.1.call-start
  168.7 43.9 %all-gather.5.cloned.1.call-done = f32[2,1,128,2048]{2,3,0,1:T(8,128)} async-done(((f32[2,1,128,256]{2,3,0,1:T(8,128)}), f32[2,1,128,2048]{2,3,0,1:T(8,128)}) %all-gather.5.cloned.1.call-update) | async-done | bytes 2097168 | tf_op jit(solution)/shard_map/all_gather | solution.py:55
  212.6 1.7 copy.45
  214.3 32.0 %all-gather.9.cloned.1.call-done = f32[2,1024,2,512]{3,1,2,0:T(8,128)} async-done(((f32[1,1024,2,512]{3,1,2,0:T(8,128)}), f32[2,1024,2,512]{3,1,2,0:T(8,128)}) %all-gather.9.cloned.1.call-update) | async-done | bytes 8388624 | tf_op jit(solution)/shard_map/all_gather | solution.py:64
  246.3 14.4 %copy.47 = f32[2,1024,2,512]{3,2,1,0:T(2,128)S(1)} copy(f32[2,1024,2,512]{3,1,2,0:T(8,128)} %all-gather.9.cloned.1.call-done) | data formatting | bytes 16777216 | tf_op jit(solution)/shard_map/all_gather | solution.py:64
  260.7 5.3 %copy.57 = f32[256,8,2,512]{3,1,2,0:T(8,128)} copy(f32[256,8,2,512]{3,2,1,0:T(2,128)S(1)} %bitcast.66) | data formatting | bytes 16777216
  266.0 9.2 %copy.48 = f32[1024,2048]{1,0:T(8,128)} copy(f32[1024,2048]{0,1:T(8,128)} %bitcast.67) | data formatting | bytes 16777216 | tf_op jit(solution)/shard_map/fak,fkb->fab/dot_general | solution.py:66
  275.3 15.8 %convolution_bitcast_fusion = f32[1,2,128,2,512]{4,2,3,1,0:T(8,128)S(1)} fusion(f32[2,128,2048,1]{1,2,3,0:T(8,128)S(1)} %bitcast.68, f32[2,512,2048,1]{2,1,0,3:T(8,128)} %bitcast.65), kind=kOutput, calls=%fused_computation.1 | convolution fusion | flops 6442450944 | bytes 11534336 | tf_op jit(solution)/shard_map/fak,fkb->fab/dot_general | solution.py:66
  291.2 0.8 pad_maximum_fusion
  292.2 0.6 fusion.6
  292.8 0.2 gather.11
  293.1 22.8 %reduce-scatter.2.cloned.1.call-done = f32[2,1,128,256]{3,2,1,0:T(8,128)} async-done(((f32[2,1,128,512]{3,2,1,0:T(8,128)}), f32[2,1,128,256]{3,2,1,0:T(8,128)}) %reduce-scatter.2.cloned.1.call-update) | async-done | bytes 262160 | tf_op jit(solution)/shard_map/reduce_scatter | solution.py:71
  315.9 2.3 slice_subtract_fusion.2
  318.2 0.7 pad_maximum_fusion.1
  (32 shorter events, 1.2 us)
Async XLA Ops:
  6.5 21.5 %copy-start = (f32[2,1,128,512]{3,2,1,0:T(8,128)S(1)}, f32[2,1,128,512]{3,2,1,0:T(8,128)}, u32[]{:S(2)}) copy-start(f32[2,1,128,512]{3,2,1,0:T(8,128)} %param.4) | copy-start | bytes 1572868
  6.5 21.8 %copy-start.2 = (s32[1,24]{1,0:T(1,128)S(1)}, s32[1,24]{1,0:T(1,128)}, u32[]{:S(2)}) copy-start(s32[1,24]{1,0:T(1,128)} %param.6) | copy-start | bytes 292
  6.5 161.9 %all-gather.7.cloned.1.call-start = ((), (), s32[]{:S(2)}) async-start(), calls=%async_computation.2 | async-start | bytes 4456448 | tf_op jit(solution)/shard_map/all_gather | solution.py:63
  8.4 12.5 %collective-permute-start.3 = (f32[2,1,128,128]{2,3,0,1:T(8,128)S(1)}, f32[2,1,128,128]{2,3,0,1:T(8,128)S(1)}, u32[]{:S(2)}, u32[]{:S(2)}) collective-permute-start(f32[2,1,128,128]{2,3,0,1:T(8,128)S(1)} %bitcast.75), channel_id=1, source_target_pairs={{16,0},{32,16},{48,32},{64,50},{80,2},{82,66},{96,18},{98,82},{112... | collective-permute-start | bytes 393224 | tf_op jit(solution)/shard_map/ppermute | solution.py:40
  17.3 3.7 %collective-permute-start.1 = (f32[2,1,128,128]{2,3,0,1:T(8,128)S(1)}, f32[2,1,128,128]{2,3,0,1:T(8,128)S(1)}, u32[]{:S(2)}, u32[]{:S(2)}) collective-permute-start(f32[2,1,128,128]{2,3,0,1:T(8,128)S(1)} %bitcast.76), channel_id=1, source_target_pairs={{48,0},{64,18},{80,34},{96,50},{112,2},{114,66},{128,20},{130,84},... | collective-permute-start | bytes 393224 | tf_op jit(solution)/shard_map/ppermute | solution.py:40
  18.1 7.0 %collective-permute-start.2 = (f32[2,1,128,128]{2,3,0,1:T(8,128)S(1)}, f32[2,1,128,128]{2,3,0,1:T(8,128)S(1)}, u32[]{:S(2)}, u32[]{:S(2)}) collective-permute-start(f32[2,1,128,128]{2,3,0,1:T(8,128)S(1)} %bitcast.77), channel_id=1, source_target_pairs={{32,0},{48,16},{64,34},{80,50},{96,2},{98,66},{112,18},{114,82},{1... | collective-permute-start | bytes 393224 | tf_op jit(solution)/shard_map/ppermute | solution.py:40
  19.5 5.6 %collective-permute-start = (f32[2,1,128,128]{2,3,0,1:T(8,128)S(1)}, f32[2,1,128,128]{2,3,0,1:T(8,128)S(1)}, u32[]{:S(2)}, u32[]{:S(2)}) collective-permute-start(f32[2,1,128,128]{2,3,0,1:T(8,128)S(1)} %bitcast.78), channel_id=1, source_target_pairs={{64,2},{80,18},{96,34},{112,50},{128,4},{130,68},{144,20},{146,84}... | collective-permute-start | bytes 393224 | tf_op jit(solution)/shard_map/ppermute | solution.py:40
  28.0 184.5 %all-gather.5.cloned.1.call-start = ((), (), s32[]{:S(2)}) async-start(), calls=%async_computation.1 | async-start | bytes 2359296 | tf_op jit(solution)/shard_map/all_gather | solution.py:55
  29.8 216.5 %all-gather.9.cloned.1.call-start = ((), (), s32[]{:S(2)}) async-start(), calls=%async_computation.4 | async-start | bytes 12582912 | tf_op jit(solution)/shard_map/all_gather | solution.py:64
  168.5 147.5 %reduce-scatter.2.cloned.1.call-start = ((), (), s32[]{:S(2)}) async-start(), calls=%async_computation.3 | async-start | bytes 786432 | tf_op jit(solution)/shard_map/reduce_scatter | solution.py:71
  275.3 16.9 %copy-start.1 = (f32[2,1]{0,1:T(1,128)S(1)}, f32[2,1]{0,1:T(1,128)}, u32[]{:S(2)}) copy-start(f32[2,1]{0,1:T(1,128)} %param.7) | copy-start | bytes 28
Sparse Core Ops, SparseCore 0:
  28.2 140.2 all-gather.6
  170.5 42.0 all-gather.4
  214.7 31.5 all-gather.8
  292.1 23.7 reduce-scatter.1
where the time goes:
time: 326 us; the launch traced here: 325 us
  waiting for transfers between devices  241 us (74%)
  local copies, waits for them, and re-layouts  35.6 us (11%)
  matrix products  15.8 us (5%)
  between operations  13.4 us (4%)
  starting transfers between devices  11.7 us (4%)
  other arithmetic  7.52 us (2%)
    all_gather x1, waiting for transfers between devices, per_device(): right = lax.all_gather(right, ('y', 'xl'), axis=1, tiled=True)  139 us
    all_gather x1, waiting for transfers between devices, per_device(): left = lax.all_gather(left, 'z', axis=3, tiled=True)  43.9 us
    all_gather x1, waiting for transfers between devices, per_device(): right = lax.all_gather(right, 'c', axis=1, tiled=False)  32 us
    reduce_scatter x1, waiting for transfers between devices, per_device(): lax.psum_scatter(partial_sum, 'xh', scatter_dimension=3, tiled=True)  22.8 us
    dot_general x1, matrix products, per_device(): jnp.einsum('fak,fkb->fab', left, right, precision=lax.Precision.HIGHEST)  15.8 us
    all_gather x1, local copies, waits for them, and re-layouts, per_device(): right = lax.all_gather(right, 'c', axis=1, tiled=False)  14.4 us
    ppermute x4, starting transfers between devices, per_device(): got = lax.ppermute(sent, FILL, mirror_pairs(n_src, n_rcv, per_rcv, step))  11.4 us
    dot_general x1, local copies, waits for them, and re-layouts, per_device(): jnp.einsum('fak,fkb->fab', left, right, precision=lax.Precision.HIGHEST)  9.22 us
  transfers between devices with their start and end apart: 8, of which 5 were waited for; matrix products, arithmetic and copies ran while one was open for 2% of the time, Pallas kernels for 0%

commit v1 on v0

--- a/solution.py
+++ b/solution.py
@@ -8,6 +8,11 @@
 TILE = 128
 SRC = ("y", "xl", "c")
 FILL = ("y", "xl", "c", "z")
+
+
+def all_by_exchange(shard, axis, dim):
+    repeated = jnp.stack([shard] * lax.axis_size(axis))
+    return jnp.concatenate(lax.all_to_all(repeated, axis, 0, 0), axis=dim)
 
 
 def mirror_pairs(n_src, n_rcv, per_rcv, step):
@@ -52,7 +57,7 @@
     left = lax.dynamic_index_in_dim(left, my_half, 4, keepdims=False)
     left = left * chosen[None, None, None, :, None]
     left = left.reshape(comp_count, freq_count, TILE, per_rcv * half)
-    left = lax.all_gather(left, "z", axis=3, tiled=True)
+    left = all_by_exchange(left, "z", 3)
     n_pair = n_src // n_core
     left = left.reshape(comp_count, freq_count, TILE, n_pair, n_core, half)
     left = jnp.transpose(left, (1, 0, 2, 4, 3, 5))

time: 326 us -> 303 us (0.929)
  waiting for transfers between devices: 241 us -> 166 us
  blocking collectives: 0 us -> 56 us
    all_to_all x0 -> x1, blocking collectives: none -> 56 us  [all_by_exchange(): return jnp.concatenate(lax.all_to_all(repeated, axis, 0, 0), axis=dim)]
    all_gather x1 -> x0, waiting for transfers between devices: 43.9 us -> none  [per_device(): left = lax.all_gather(left, 'z', axis=3, tiled=True)]
    all_gather x1, waiting for transfers between devices: 32 us -> 0.02 us  [per_device(): right = lax.all_gather(right, 'c', axis=1, tiled=False)]
  transfers between devices with their start and end apart: 8 -> 7, of which waited for: 5 -> 3; matrix products, arithmetic and copies ran while one was open for 2% -> 1% of each run, Pallas kernels for 0% -> 0%
where the time goes in v1:
time: 303 us
  waiting for transfers between devices  166 us (55%)
  blocking collectives  56 us (18%)
  local copies, waits for them, and re-layouts  34.4 us (11%)
  matrix products  15.8 us (5%)
  between operations  13.4 us (4%)
  starting transfers between devices  11.5 us (4%)
  other arithmetic  5.9 us (2%)
    all_gather x1, waiting for transfers between devices, per_device(): right = lax.all_gather(right, ('y', 'xl'), axis=1, tiled=True)  140 us
    all_to_all x1, blocking collectives, all_by_exchange(): return jnp.concatenate(lax.all_to_all(repeated, axis, 0, 0), axis=dim)  56 us
    reduce_scatter x1, waiting for transfers between devices, per_device(): lax.psum_scatter(partial_sum, 'xh', scatter_dimension=3, tiled=True)  21.4 us
    dot_general x1, matrix products, per_device(): jnp.einsum('fak,fkb->fab', left, right, precision=lax.Precision.HIGHEST)  15.8 us
    all_gather x1, local copies, waits for them, and re-layouts, per_device(): right = lax.all_gather(right, 'c', axis=1, tiled=False)  14.4 us
    ppermute x4, starting transfers between devices, per_device(): got = lax.ppermute(sent, FILL, mirror_pairs(n_src, n_rcv, per_rcv, step))  11.4 us
    dot_general x1, local copies, waits for them, and re-layouts, per_device(): jnp.einsum('fak,fkb->fab', left, right, precision=lax.Precision.HIGHEST)  9.13 us
  transfers between devices with their start and end apart: 7, of which 3 were waited for; matrix products, arithmetic and copies ran while one was open for 1% of the time, Pallas kernels for 0%

profile of v1, /device:TPU:1, one launch (start us, length us, event | category | flops | bytes accessed | tf_op | source)
XLA Modules:
  0.0 303.0 jit_solution(50450297979556376)
XLA Ops:
  6.5 1.3 reshape.246
  7.8 0.5 constant_dynamic-slice_fusion.3
  8.4 8.8 %collective-permute-start.3 = (f32[2,1,128,128]{2,3,0,1:T(8,128)S(1)}, f32[2,1,128,128]{2,3,0,1:T(8,128)S(1)}, u32[]{:S(2)}, u32[]{:S(2)}) collective-permute-start(f32[2,1,128,128]{2,3,0,1:T(8,128)S(1)} %bitcast.77), channel_id=1, source_target_pairs={{16,0},{32,16},{48,32},{64,50},{80,2},{82,66},{96,18},{98,82},{112... | collective-permute-start | bytes 393224 | tf_op jit(solution)/shard_map/ppermute | solution.py:45
  17.3 0.7 collective-permute-start.1
  18.1 1.3 collective-permute-start.2
  19.5 0.7 collective-permute-start
  20.2 0.7 compare_bitcast_fusion
  21.0 4.1 %collective-permute-done.2 = f32[2,1,128,128]{2,3,0,1:T(8,128)S(1)} collective-permute-done((f32[2,1,128,128]{2,3,0,1:T(8,128)S(1)}, f32[2,1,128,128]{2,3,0,1:T(8,128)S(1)}, u32[]{:S(2)}, u32[]{:S(2)}) %collective-permute-start.2) | collective-permute-done | bytes 131104 | tf_op jit(solution)/shard_map/ppermute | solution.py:45
  25.1 0.6 gather_fusion
  25.7 0.3 copy.43
  26.1 0.2 gather.13
  26.3 0.7 fusion.2
  27.1 140.3 %all-gather.4.cloned.1.call-done = f32[1,1024,2,512]{3,1,2,0:T(8,128)} async-done(((f32[1,64,2,512]{3,1,2,0:T(8,128)}), f32[1,1024,2,512]{3,1,2,0:T(8,128)}) %all-gather.4.cloned.1.call-update) | async-done | bytes 4194320 | tf_op jit(solution)/shard_map/all_gather | solution.py:68
  167.6 0.2 copy.45
  167.8 0.2 convert_reduce_fusion
  168.1 0.2 copy.44
  168.3 0.1 dynamic-slice_select_fusion.2
  168.4 0.1 broadcast_multiply_fusion
  168.5 0.2 stack.33
  168.8 56.0 %all_to_all.5 = f32[8,2,1,128,256]{3,4,1,2,0:T(8,128)S(1)} all-to-all(f32[8,2,1,128,256]{3,4,1,2,0:T(8,128)S(1)} %stack.33), channel_id=1, replica_groups=mesh['y'=8,'xl'=2,'c'=2,'z'=8,'xh'=2] {'z'}, dimensions={0} | all-to-all | bytes 4194304 | tf_op jit(solution)/shard_map/all_to_all | solution.py:15
  224.8 0.2 copy.46
  225.0 0.2 copy.47
  225.3 14.4 %copy.49 = f32[2,1024,2,512]{3,2,1,0:T(2,128)S(1)} copy(f32[2,1024,2,512]{3,1,2,0:T(8,128)} %all-gather.6.cloned.1.call-done) | data formatting | bytes 16777216 | tf_op jit(solution)/shard_map/all_gather | solution.py:69
  239.7 5.3 %copy.59 = f32[256,8,2,512]{3,1,2,0:T(8,128)} copy(f32[256,8,2,512]{3,2,1,0:T(2,128)S(1)} %bitcast.67) | data formatting | bytes 16777216
  245.0 9.1 %copy.50 = f32[1024,2048]{1,0:T(8,128)} copy(f32[1024,2048]{0,1:T(8,128)} %bitcast.68) | data formatting | bytes 16777216 | tf_op jit(solution)/shard_map/fak,fkb->fab/dot_general | solution.py:71
  254.1 15.8 %convolution_bitcast_fusion = f32[1,2,128,2,512]{4,2,3,1,0:T(8,128)S(1)} fusion(f32[2,128,2048,1]{1,2,3,0:T(8,128)S(1)} %bitcast.70, f32[2,512,2048,1]{2,1,0,3:T(8,128)} %bitcast.66), kind=kOutput, calls=%fused_computation.1 | convolution fusion | flops 6442450944 | bytes 11534336 | tf_op jit(solution)/shard_map/fak,fkb->fab/dot_general | solution.py:71
  270.0 0.8 pad_maximum_fusion
  271.0 0.7 fusion.6
  271.7 0.2 gather.11
  272.0 21.4 %reduce-scatter.2.cloned.1.call-done = f32[2,1,128,256]{3,2,1,0:T(8,128)} async-done(((f32[2,1,128,512]{3,2,1,0:T(8,128)}), f32[2,1,128,256]{3,2,1,0:T(8,128)}) %reduce-scatter.2.cloned.1.call-update) | async-done | bytes 262160 | tf_op jit(solution)/shard_map/reduce_scatter | solution.py:76
  293.4 2.3 slice_subtract_fusion.2
  295.8 0.7 pad_maximum_fusion.1
  (32 shorter events, 1.2 us)
Async XLA Ops:
  6.5 19.8 %copy-start = (f32[2,1,128,512]{3,2,1,0:T(8,128)S(1)}, f32[2,1,128,512]{3,2,1,0:T(8,128)}, u32[]{:S(2)}) copy-start(f32[2,1,128,512]{3,2,1,0:T(8,128)} %param.4) | copy-start | bytes 1572868
  6.5 161.0 %all-gather.4.cloned.1.call-start = ((), (), s32[]{:S(2)}) async-start(), calls=%async_computation.2 | async-start | bytes 4456448 | tf_op jit(solution)/shard_map/all_gather | solution.py:68
  8.4 12.5 %collective-permute-start.3 = (f32[2,1,128,128]{2,3,0,1:T(8,128)S(1)}, f32[2,1,128,128]{2,3,0,1:T(8,128)S(1)}, u32[]{:S(2)}, u32[]{:S(2)}) collective-permute-start(f32[2,1,128,128]{2,3,0,1:T(8,128)S(1)} %bitcast.77), channel_id=1, source_target_pairs={{16,0},{32,16},{48,32},{64,50},{80,2},{82,66},{96,18},{98,82},{112... | collective-permute-start | bytes 393224 | tf_op jit(solution)/shard_map/ppermute | solution.py:45
  17.3 3.7 %collective-permute-start.1 = (f32[2,1,128,128]{2,3,0,1:T(8,128)S(1)}, f32[2,1,128,128]{2,3,0,1:T(8,128)S(1)}, u32[]{:S(2)}, u32[]{:S(2)}) collective-permute-start(f32[2,1,128,128]{2,3,0,1:T(8,128)S(1)} %bitcast.78), channel_id=1, source_target_pairs={{48,0},{64,18},{80,34},{96,50},{112,2},{114,66},{128,20},{130,84},... | collective-permute-start | bytes 393224 | tf_op jit(solution)/shard_map/ppermute | solution.py:45
  18.1 7.0 %collective-permute-start.2 = (f32[2,1,128,128]{2,3,0,1:T(8,128)S(1)}, f32[2,1,128,128]{2,3,0,1:T(8,128)S(1)}, u32[]{:S(2)}, u32[]{:S(2)}) collective-permute-start(f32[2,1,128,128]{2,3,0,1:T(8,128)S(1)} %bitcast.79), channel_id=1, source_target_pairs={{32,0},{48,16},{64,34},{80,50},{96,2},{98,66},{112,18},{114,82},{1... | collective-permute-start | bytes 393224 | tf_op jit(solution)/shard_map/ppermute | solution.py:45
  19.5 5.6 %collective-permute-start = (f32[2,1,128,128]{2,3,0,1:T(8,128)S(1)}, f32[2,1,128,128]{2,3,0,1:T(8,128)S(1)}, u32[]{:S(2)}, u32[]{:S(2)}) collective-permute-start(f32[2,1,128,128]{2,3,0,1:T(8,128)S(1)} %bitcast.80), channel_id=1, source_target_pairs={{64,2},{80,18},{96,34},{112,50},{128,4},{130,68},{144,20},{146,84}... | collective-permute-start | bytes 393224 | tf_op jit(solution)/shard_map/ppermute | solution.py:45
  25.7 142.0 %copy-start.2 = (s32[1,24]{1,0:T(1,128)S(1)}, s32[1,24]{1,0:T(1,128)}, u32[]{:S(2)}) copy-start(s32[1,24]{1,0:T(1,128)} %param.6) | copy-start | bytes 292
  27.1 198.2 %all-gather.6.cloned.1.call-start = ((), (), s32[]{:S(2)}) async-start(), calls=%async_computation.4 | async-start | bytes 12582912 | tf_op jit(solution)/shard_map/all_gather | solution.py:69
  167.5 125.9 %reduce-scatter.2.cloned.1.call-start = ((), (), s32[]{:S(2)}) async-start(), calls=%async_computation.3 | async-start | bytes 786432 | tf_op jit(solution)/shard_map/reduce_scatter | solution.py:76
  254.1 16.9 %copy-start.1 = (f32[2,1]{0,1:T(1,128)S(1)}, f32[2,1]{0,1:T(1,128)}, u32[]{:S(2)}) copy-start(f32[2,1]{0,1:T(1,128)} %param.7) | copy-start | bytes 28
Sparse Core Ops, SparseCore 0:
  27.2 140.2 all-gather.3
  169.6 30.8 all-gather.5
  271.0 22.3 reduce-scatter.1
